TPU v7x, 256 devices: a whole 4x4x8 slice. The times are simulated.
256 devices in a mesh: dp: 8 (over z), seq: 32 (over x, y, core).
Axes of the slice: x: 4, y: 4, z: 8, core: 2. Of those that a mesh axis runs over, the one named last changes fastest.
Arguments:
- inputs: bfloat16 [8, 8192, 5120], P('dp', 'seq'), may hold values from -6 to 6
- gate_proj: bfloat16 [8, 8192, 5120], P('dp', 'seq'), may hold values from -6 to 6
- write_proj: bfloat16 [8, 8192, 128], P('dp', 'seq'), may hold values from -6 to 6
- read_proj: bfloat16 [8, 8192, 128], P('dp', 'seq'), may hold values from -6 to 6
- step_size: float32 [8, 80, 8192], P('dp', None, 'seq'), may hold values from 0 to 0.4, as said below
- log_forget: float32 [8, 80, 8192], P('dp', None, 'seq'), may hold values from -0.8 to 0, as said below
- conv_weight: float32 [4, 5376], replicated, may hold values from -3 to 3
- conv_bias: float32 [5376], replicated, may hold values from -3 to 3
- skip_gain: float32 [80], replicated, may hold values from 0.5 to 1.5
- norm_gain: float32 [5120], replicated, may hold values from 0.1 to 1.9
- code_weight: bfloat16 [5120, 256], P('dp'), may hold values from -0.5 to 0.5
- prior_draw: float32 [2048, 256], P(('dp', 'seq')), may hold values from -6 to 6
Outputs:
- mixed: bfloat16 [8, 8192, 5120], P('dp', 'seq')
- codes: float32 [2048, 256], P(('dp', 'seq'))
- kernel: float32 [2048, 4096], P(('dp', 'seq'))
Inputs may be any that keep to these rules, and one draw needn't show every extreme that they name: `step_size`: positive step sizes, per document, head and position. `log_forget`: never positive.
All inputs are finite; a program needn't handle non-finite values.
Results may differ from a plain program's by a relative error of at most 0.008.
Values may be sent and summed in bfloat16 or wider, within the bound.
No kernel may reach another device: no remote copies, remote signals or barrier semaphores. Data moves between devices by JAX's collectives and lax.ppermute only.
A program may use at most 256 MiB of HBM per device.

v0:
```python
import jax
import jax.numpy as jnp
from jax import lax
from jax.sharding import PartitionSpec as P

SPAN = 128
SEG = 32


def passed_along(block, axis, distance):
    devices = range(lax.axis_size(axis))
    route = [(i - distance, i) for i in devices if i - distance in devices]
    return lax.ppermute(block, axis, route)


def carried_in(part, axis, combine, identity):
    place = lax.axis_index(axis)
    gathered = jax.tree.map(lambda a: lax.all_gather(a, axis), part)
    state = jax.tree.map(lambda a, e: jnp.zeros_like(a) + jnp.asarray(e, a.dtype), part, identity)

    def one(step, state):
        return combine(
            state, jax.tree.map(lambda a: lax.dynamic_index_in_dim(a, step, 0, False), gathered)
        )

    return lax.fori_loop(0, place, one, state)


def block_terms(values, write_rows, read_rows, steps, logs):
    cum_log = jnp.cumsum(logs, axis=1)
    length = logs.shape[1]
    causal = jnp.arange(length)[:, None] >= jnp.arange(length)[None, :]
    scores = jnp.dot(read_rows, write_rows.T, preferred_element_type=jnp.float32)
    decay = jnp.exp(jnp.where(causal[None], cum_log[:, :, None] - cum_log[:, None, :], -jnp.inf))
    mixing = (scores[None] * decay * steps[:, None, :]).astype(jnp.bfloat16)
    inner_out = jnp.einsum("hts,shp->thp", mixing, values, preferred_element_type=jnp.float32)
    tail_decay = jnp.exp(cum_log[:, -1:] - cum_log) * steps
    weighted = (tail_decay[:, :, None] * write_rows.astype(jnp.float32)[None]).astype(jnp.bfloat16)
    states = jnp.einsum("hsn,shp->hpn", weighted, values, preferred_element_type=jnp.float32)
    return (inner_out, states, cum_log)


def join_states(first, second):
    return (first[0] + second[0], jnp.exp(second[0])[:, None, None] * first[1] + second[1])


def per_device(
    inputs,
    gate_proj,
    write_proj,
    read_proj,
    step_size,
    log_forget,
    conv_weight,
    conv_bias,
    skip_gain,
    norm_gain,
    code_weight,
    prior_draw,
):
    length = inputs.shape[1]
    width = inputs.shape[2]
    state_dim = write_proj.shape[2]
    heads = step_size.shape[1]
    head_dim = width // heads
    taps = conv_weight.shape[0]
    joined = jnp.concatenate([inputs[0], write_proj[0], read_proj[0]], axis=1)
    rim_rows = passed_along(joined[length - (taps - 1) :], "seq", 1)
    padded = jnp.concatenate([rim_rows, joined], axis=0)
    summed = conv_bias[None, :] + conv_weight[0][None, :] * padded[0:length].astype(jnp.float32)
    for offset in range(1, taps):
        summed = summed + conv_weight[offset][None, :] * padded[offset : offset + length].astype(
            jnp.float32
        )
    active = jax.nn.silu(summed).astype(jnp.bfloat16)
    values = active[:, :width].reshape(length, heads, head_dim)
    write_all = active[:, width : width + state_dim]
    read_all = active[:, width + state_dim :]
    steps = step_size[0]
    logs = log_forget[0]
    blocks = length // SPAN
    inner_list = []
    state_list = []
    cum_list = []
    for block in range(blocks):
        lower = block * SPAN
        upper = lower + SPAN
        inner_out, states, cum_log = block_terms(
            values[lower:upper],
            write_all[lower:upper],
            read_all[lower:upper],
            steps[:, lower:upper],
            logs[:, lower:upper],
        )
        inner_list.append(inner_out)
        state_list.append(states)
        cum_list.append(cum_log)
    running = jnp.zeros((heads, head_dim, state_dim), jnp.float32)
    before = jnp.zeros((heads,), jnp.float32)
    start_list = []
    before_list = []
    for block in range(blocks):
        start_list.append(running)
        before_list.append(before)
        block_total = cum_list[block][:, -1]
        running = jnp.exp(block_total)[:, None, None] * running + state_list[block]
        before = before + block_total
    identity = (jnp.zeros_like(before), jnp.zeros_like(running))
    decay_in, carry_in = carried_in((before, running), "seq", join_states, identity)
    outputs = []
    for block in range(blocks):
        lower = block * SPAN
        upper = lower + SPAN
        start = start_list[block] + jnp.exp(before_list[block])[:, None, None] * carry_in
        read_block = read_all[lower:upper].astype(jnp.float32)
        outer_out = jnp.exp(cum_list[block]).T[:, :, None] * jnp.einsum(
            "tn,hpn->thp", read_block, start, precision=lax.Precision.HIGHEST
        )
        outputs.append(inner_list[block] + outer_out)
    ssd_out = jnp.concatenate(outputs, axis=0)
    total = ssd_out + skip_gain[None, :, None] * values.astype(jnp.float32)
    gated = total.reshape(length, width) * jax.nn.silu(gate_proj[0].astype(jnp.float32))
    scale = lax.rsqrt(jnp.mean(gated * gated, axis=1, keepdims=True) + 1e-05)
    mixed = (gated * scale * norm_gain[None, :]).astype(jnp.bfloat16)
    pooled = jnp.mean(mixed.astype(jnp.float32).reshape(length // SEG, SEG, width), axis=1).astype(
        jnp.bfloat16
    )
    codes_local = jnp.dot(
        pooled,
        lax.all_gather(code_weight, "dp", axis=0, tiled=True),
        preferred_element_type=jnp.float32,
    )
    all_codes, all_prior = (
        lax.all_gather(codes_local, ("dp", "seq"), axis=0, tiled=True),
        lax.all_gather(prior_draw, ("dp", "seq"), axis=0, tiled=True),
    )
    columns = jnp.concatenate([all_codes, all_prior], axis=0)
    cross = jnp.dot(codes_local, columns.T, precision=lax.Precision.HIGHEST)
    row_sq = jnp.sum(codes_local * codes_local, axis=1)
    col_sq = jnp.sum(columns * columns, axis=1)
    dist_sq = row_sq[:, None] + col_sq[None, :] - 2.0 * cross
    code_dim = codes_local.shape[1]
    kernel = 2.0 * code_dim / (2.0 * code_dim + dist_sq)
    return (mixed[None], codes_local, kernel)


def solution(mesh):
    in_specs = (
        P("dp", "seq", None),
        P("dp", "seq", None),
        P("dp", "seq", None),
        P("dp", "seq", None),
        P("dp", None, "seq"),
        P("dp", None, "seq"),
        P(),
        P(),
        P(),
        P(),
        P("dp", None),
        P(("dp", "seq"), None),
    )
    out_specs = (P("dp", "seq", None), P(("dp", "seq"), None), P(("dp", "seq"), None))
    return jax.shard_map(
        per_device, mesh=mesh, in_specs=in_specs, out_specs=out_specs, check_vma=False
    )
```

profile of v0, /device:TPU:1, one launch (start us, length us, event | category | flops | bytes accessed | tf_op | source)
XLA Modules:
  0.0 618.8 jit_solution(9493338200007290373)
XLA Ops:
  9.5 4.6 collective-permute-start
  17.7 4.4 multiply_convert_fusion
  24.2 2.4 copy.31
  29.0 3.9 fusion.9
  34.4 4.0 multiply_add_fusion
  40.9 126.3 %all-reduce = f32[2560]{0:T(1024)S(1)} all-reduce(f32[2560]{0:T(1024)S(1)} %dynamic-update-slice), channel_id=2, replica_groups=mesh['dp'=8,'seq'=32] {'seq'}, use_global_device_ids=true, to_apply=%add | all-reduce | flops 2560 | bytes 20480
  167.5 4.5 fusion.7
  172.2 4.1 fusion.8
  176.2 116.8 %all-gather.13.cloned.1.call-done = f32[2560,64,128]{2,1,0:T(8,128)} async-done(((f32[80,64,128]{2,1,0:T(8,128)}), f32[2560,64,128]{2,1,0:T(8,128)}) %all-gather.13.cloned.1.call-update) | async-done | bytes 83886096 | tf_op jit(solution)/shard_map/all_gather | solution.py:18
  293.4 2.4 while.12
  295.8 4.6 bitcast_add_fusion.2
  300.4 3.2 copy.37
  303.6 5.7 bitcast_add_fusion.1
  309.3 3.4 copy.38
  312.7 5.3 multiply_reduce_fusion
  321.3 11.0 %all-gather.7.cloned.1.call-done = bf16[5120,256]{1,0:T(8,128)(2,1)} async-done(((bf16[640,256]{1,0:T(8,128)(2,1)}), bf16[5120,256]{1,0:T(8,128)(2,1)}) %all-gather.7.cloned.1.call-update) | async-done | bytes 2621456 | tf_op jit(solution)/shard_map/all_gather | solution.py:130
  332.3 2.9 multiply_reduce_fusion.2
  335.8 4.7 fusion.50
  340.5 154.3 %all-gather.9.cloned.1.call-done = f32[2048,256]{1,0:T(8,128)} async-done(((f32[8,256]{1,0:T(8,128)}), f32[2048,256]{1,0:T(8,128)}) %all-gather.9.cloned.1.call-update) | async-done | bytes 2097168 | tf_op jit(solution)/shard_map/all_gather | solution.py:134
  494.8 3.1 constant_dynamic-update-slice_fusion.1
  497.9 103.6 %all-gather.11.cloned.1.call-done = f32[2048,256]{1,0:T(8,128)} async-done(((f32[8,256]{1,0:T(8,128)}), f32[2048,256]{1,0:T(8,128)}) %all-gather.11.cloned.1.call-update) | async-done | bytes 2097168 | tf_op jit(solution)/shard_map/all_gather | solution.py:135
  601.5 3.0 constant_dynamic-update-slice_fusion
  604.6 3.0 multiply_reduce_fusion.1
  608.0 4.2 fusion.6
  (75 shorter events, 20.7 us)
Async XLA Ops:
  7.2 285.9 %all-gather.13.cloned.1.call-start = ((), (), s32[]{:S(2)}) async-start(), calls=%async_computation.3 | async-start | bytes 86507520 | tf_op jit(solution)/shard_map/all_gather | solution.py:18
  7.2 6.8 %copy-start.13 = (f32[1,80,256]{2,1,0:T(8,128)S(1)}, f32[1,80,256]{2,1,0:T(8,128)}, u32[]{:S(2)}) copy-start(f32[1,80,256]{2,1,0:T(8,128)} %param.19) | copy-start | bytes 245764
  7.2 7.7 %copy-start.14 = (f32[1,80,256]{2,1,0:T(8,128)S(1)}, f32[1,80,256]{2,1,0:T(8,128)}, u32[]{:S(2)}) copy-start(f32[1,80,256]{2,1,0:T(8,128)} %param.18) | copy-start | bytes 245764
  7.2 7.8 %copy-start.11 = (f32[4,5376]{1,0:T(4,128)S(1)}, f32[4,5376]{1,0:T(4,128)}, u32[]{:S(2)}) copy-start(f32[4,5376]{1,0:T(4,128)} %param.20) | copy-start | bytes 258052
  7.2 8.1 %copy-start.4 = (bf16[1,256,5120]{2,1,0:T(8,128)(2,1)S(1)}, bf16[1,256,5120]{2,1,0:T(8,128)(2,1)}, u32[]{:S(2)}) copy-start(bf16[1,256,5120]{2,1,0:T(8,128)(2,1)} %param.14) | copy-start | bytes 7864324
  7.3 8.1 %copy-start.9 = (bf16[1,256,128]{2,1,0:T(8,128)(2,1)S(1)}, bf16[1,256,128]{2,1,0:T(8,128)(2,1)}, u32[]{:S(2)}) copy-start(bf16[1,256,128]{2,1,0:T(8,128)(2,1)} %param.17) | copy-start | bytes 196612
  7.3 8.1 %copy-start.10 = (bf16[1,256,128]{2,1,0:T(8,128)(2,1)S(1)}, bf16[1,256,128]{2,1,0:T(8,128)(2,1)}, u32[]{:S(2)}) copy-start(bf16[1,256,128]{2,1,0:T(8,128)(2,1)} %param.16) | copy-start | bytes 196612
  9.5 5.8 collective-permute-start
  15.3 2.4 copy-start.5
  15.3 2.4 copy-start.16
  22.2 149.9 %copy-start.2 = (bf16[256,5376]{1,0:T(8,128)(2,1)}, bf16[256,5376]{1,0:T(8,128)(2,1)S(1)}, u32[]{:S(2)}) copy-start(bf16[256,5376]{1,0:T(8,128)(2,1)S(1)} %multiply_convert_fusion) | copy-start | bytes 8257540
  29.0 5.4 copy-start.7
  33.0 1.5 copy-start.6
  38.5 0.9 copy-start.18
  38.5 128.8 %copy-start.17 = (f32[80]{0:T(128)S(1)}, f32[80]{0:T(128)}, u32[]{:S(2)}) copy-start(f32[80]{0:T(128)} %param.22) | copy-start | bytes 964
  38.5 293.8 %all-gather.7.cloned.1.call-start = ((), (), s32[]{:S(2)}) async-start(), calls=%async_computation | async-start | bytes 2949120 | tf_op jit(solution)/shard_map/all_gather | solution.py:130
  39.3 455.6 %all-gather.9.cloned.1.call-start = ((), (), s32[]{:S(2)}) async-start(), calls=%async_computation.1 | async-start | bytes 2105344 | tf_op jit(solution)/shard_map/all_gather | solution.py:134
  167.5 4.7 copy-start.8
  309.3 3.4 copy-start.3
  312.7 7.6 %copy-start.12 = (f32[5120]{0:T(1024)S(1)}, f32[5120]{0:T(1024)}, u32[]{:S(2)}) copy-start(f32[5120]{0:T(1024)} %param.23) | copy-start | bytes 61444
  318.0 2.3 copy-start
  335.3 266.3 %all-gather.11.cloned.1.call-start = ((), (), s32[]{:S(2)}) async-start(), calls=%async_computation.2 | async-start | bytes 2105344 | tf_op jit(solution)/shard_map/all_gather | solution.py:135
  604.6 3.4 copy-start.1
  604.6 3.4 copy-start.15
Sparse Core Ops, SparseCore 0:
  38.6 254.3 all-gather.12
  294.8 37.4 all-gather.6
  336.6 158.1 all-gather.8
  498.4 103.0 all-gather.10
where the time goes:
time: 620 us; the launch traced here: 619 us
  waiting for transfers between devices  387 us (62%)
  blocking collectives  126 us (20%)
  matrix products  34.3 us (6%)
  other arithmetic  26 us (4%)
  local copies, waits for them, and re-layouts  25.5 us (4%)
  between operations  14.8 us (2%)
    all_gather x1, waiting for transfers between devices, per_device(): lax.all_gather(codes_local, ('dp', 'seq'), axis=0, tiled=True)  154 us
    unnamed x1, blocking collectives  126 us
    all_gather x1, waiting for transfers between devices, carried_in(): gathered = jax.tree.map(lambda a: lax.all_gather(a, axis), part)  117 us
    all_gather x1, waiting for transfers between devices, per_device(): lax.all_gather(prior_draw, ('dp', 'seq'), axis=0, tiled=True)  104 us
  transfers between devices with their start and end apart: 5, of which 4 were waited for; matrix products, arithmetic and copies ran while one was open for 7% of the time, Pallas kernels for 0%

commit v1 on v0

--- a/solution.py
+++ b/solution.py
@@ -130,8 +130,20 @@
         lax.all_gather(code_weight, "dp", axis=0, tiled=True),
         preferred_element_type=jnp.float32,
     )
+
+    def expand_patches_up(xs):
+        return jnp.concatenate(
+            lax.all_to_all(
+                jnp.stack([xs for _ in range(lax.axis_size(("dp", "seq")))], axis=0),
+                axis_name=("dp", "seq"),
+                split_axis=0,
+                concat_axis=0,
+            ),
+            axis=0,
+        )
+
     all_codes, all_prior = (
-        lax.all_gather(codes_local, ("dp", "seq"), axis=0, tiled=True),
+        expand_patches_up(codes_local),
         lax.all_gather(prior_draw, ("dp", "seq"), axis=0, tiled=True),
     )
     columns = jnp.concatenate([all_codes, all_prior], axis=0)

time: 620 us -> 474 us (0.76)
  waiting for transfers between devices: 387 us -> 180 us
  starting transfers between devices: 4.74 us -> 71.5 us
    all_gather x1 -> x0, waiting for transfers between devices: 154 us -> none  [per_device(): lax.all_gather(codes_local, ('dp', 'seq'), axis=0, tiled=True)]
    all_to_all x0 -> x1, starting transfers between devices: none -> 66.8 us  [expand_patches_up(): lax.all_to_all(jnp.stack([xs for _ in range(lax.axis_size(('dp', 'seq')))...]
    all_gather x1, waiting for transfers between devices: 104 us -> 45 us  [per_device(): lax.all_gather(prior_draw, ('dp', 'seq'), axis=0, tiled=True)]
    all_to_all x0 -> x1, waiting for transfers between devices: none -> 6.76 us  [expand_patches_up(): lax.all_to_all(jnp.stack([xs for _ in range(lax.axis_size(('dp', 'seq')))...]
  transfers between devices with their start and end apart: 5 -> 5, of which waited for: 4 -> 4; matrix products, arithmetic and copies ran while one was open for 7% -> 10% of each run, Pallas kernels for 0% -> 0%
where the time goes in v1:
time: 474 us; the launch traced here: 473 us
  waiting for transfers between devices  180 us (38%)
  blocking collectives  126 us (27%)
  starting transfers between devices  71.5 us (15%)
  matrix products  33.7 us (7%)
  other arithmetic  25.4 us (5%)
  local copies, waits for them, and re-layouts  20.5 us (4%)
  between operations  14.8 us (3%)
    unnamed x1, blocking collectives  126 us
    all_gather x1, waiting for transfers between devices, carried_in(): gathered = jax.tree.map(lambda a: lax.all_gather(a, axis), part)  116 us
    all_to_all x1, starting transfers between devices, expand_patches_up(): lax.all_to_all(jnp.stack([xs for _ in range(lax.axis_size(('dp', 'seq')))...  66.8 us
    all_gather x1, waiting for transfers between devices, per_device(): lax.all_gather(prior_draw, ('dp', 'seq'), axis=0, tiled=True)  45 us
    all_gather x1, waiting for transfers between devices, per_device(): lax.all_gather(code_weight, 'dp', axis=0, tiled=True)  10.9 us
    dot_general x2, matrix products, per_device(): jnp.einsum('tn,hpn->thp', read_block, start, precision=lax.Precision.HIGH...  10.4 us
  transfers between devices with their start and end apart: 5, of which 4 were waited for; matrix products, arithmetic and copies ran while one was open for 10% of the time, Pallas kernels for 0%

profile of v1, /device:TPU:1, one launch (start us, length us, event | category | flops | bytes accessed | tf_op | source)
XLA Modules:
  0.0 472.6 jit_solution(2061476366741321254)
XLA Ops:
  9.5 4.6 collective-permute-start
  15.3 2.4 maximum_maximum_fusion
  17.7 4.4 multiply_convert_fusion
  24.2 2.4 copy.31
  26.6 2.4 copy.32
  29.0 3.9 fusion.9
  34.4 4.0 multiply_add_fusion
  41.6 126.4 %all-reduce = f32[2560]{0:T(1024)S(1)} all-reduce(f32[2560]{0:T(1024)S(1)} %dynamic-update-slice), channel_id=2, replica_groups=mesh['dp'=8,'seq'=32] {'seq'}, use_global_device_ids=true, to_apply=%add | all-reduce | flops 2560 | bytes 20480
  168.5 4.5 fusion.7
  173.0 4.0 fusion.8
  177.1 116.0 %all-gather.10.cloned.1.call-done = f32[2560,64,128]{2,1,0:T(8,128)} async-done(((f32[80,64,128]{2,1,0:T(8,128)}), f32[2560,64,128]{2,1,0:T(8,128)}) %all-gather.10.cloned.1.call-update) | async-done | bytes 83886096 | tf_op jit(solution)/shard_map/all_gather | solution.py:18
  293.4 2.4 while.12
  295.8 4.6 bitcast_add_fusion.2
  300.4 3.2 copy.37
  303.7 5.7 %bitcast_add_fusion.1 = f32[128,80,64]{0,2,1:T(8,128)} fusion(f32[80,64,128]{2,1,0:T(8,128)} %fusion.8, f32[80,64,128]{2,1,0:T(8,128)S(1)} %get-tuple-element.47, f32[80,64,128]{2,1,0:T(8,128)} %copy-done.5, f32[80]{0:T(128)S(1)} %get-tuple-element.79, f32[128,80]{0,1:T(8,128)S(1)} %get-tuple-element.77, f32[80]{0:T(128)S(1)} %get-tuple-element.80, ...), kind=kOutput, calls=%fused_computation.29 | convolution fusion | flops 1009909760 | bytes 10560128 | tf_op jit(solution)/shard_map/tn,hpn->thp/dot_general | solution.py:116
  309.4 3.4 copy.38
  312.8 5.3 %multiply_reduce_fusion = (f32[256]{0:T(256)S(1)}, f32[256,5120]{1,0:T(8,128)S(1)}) fusion(bf16[1,256,5120]{2,1,0:T(8,128)(2,1)} %param.15, bf16[256,5376]{1,0:T(8,128)(2,1)S(1)} %copy-done.2, f32[5120]{0:T(1024)S(1)} %mul.252, f32[128,5120]{1,0:T(8,128)} %copy.38, f32[128,5120]{1,0:T(8,128)} %copy.37), kind=kLoop, calls=%fused_computation.12 | loop fusion | flops 15728384 | bytes 15750144 | tf_op jit(solution)/shard_map/reduce_sum | solution.py:123
  321.4 10.9 %all-gather.6.cloned.1.call-done = bf16[5120,256]{1,0:T(8,128)(2,1)} async-done(((bf16[640,256]{1,0:T(8,128)(2,1)}), bf16[5120,256]{1,0:T(8,128)(2,1)}) %all-gather.6.cloned.1.call-update) | async-done | bytes 2621456 | tf_op jit(solution)/shard_map/all_gather | solution.py:130
  336.2 66.8 %all-to-all-start = ((f32[256,8,256]{2,1,0:T(8,128)}), f32[256,8,256]{2,1,0:T(8,128)S(1)}, u32[]{:S(2)}, u32[]{:S(2)}) async-start(f32[256,8,256]{2,1,0:T(8,128)} %stack.2), calls=%async_computation | async-start | bytes 4194304 | tf_op jit(solution)/shard_map/all_to_all | solution.py:136
  403.0 4.7 fusion.51
  407.7 45.0 %all-gather.8.cloned.1.call-done = f32[2048,256]{1,0:T(8,128)} async-done(((f32[8,256]{1,0:T(8,128)}), f32[2048,256]{1,0:T(8,128)}) %all-gather.8.cloned.1.call-update) | async-done | bytes 2097168 | tf_op jit(solution)/shard_map/all_gather | solution.py:147
  452.7 6.8 %all-to-all-done = f32[256,8,256]{2,1,0:T(8,128)S(1)} async-done(((f32[256,8,256]{2,1,0:T(8,128)}), f32[256,8,256]{2,1,0:T(8,128)S(1)}, u32[]{:S(2)}, u32[]{:S(2)}) %all-to-all-start) | async-done | bytes 2097184 | tf_op jit(solution)/shard_map/all_to_all | solution.py:136
  459.5 2.4 multiply_reduce_fusion.1
  461.9 4.2 fusion.6
  (73 shorter events, 19.4 us)
Async XLA Ops:
  7.2 285.9 %all-gather.10.cloned.1.call-start = ((), (), s32[]{:S(2)}) async-start(), calls=%async_computation.3 | async-start | bytes 86507520 | tf_op jit(solution)/shard_map/all_gather | solution.py:18
  7.2 6.8 %copy-start.13 = (f32[1,80,256]{2,1,0:T(8,128)S(1)}, f32[1,80,256]{2,1,0:T(8,128)}, u32[]{:S(2)}) copy-start(f32[1,80,256]{2,1,0:T(8,128)} %param.19) | copy-start | bytes 245764
  7.2 7.7 %copy-start.14 = (f32[1,80,256]{2,1,0:T(8,128)S(1)}, f32[1,80,256]{2,1,0:T(8,128)}, u32[]{:S(2)}) copy-start(f32[1,80,256]{2,1,0:T(8,128)} %param.18) | copy-start | bytes 245764
  7.2 7.8 %copy-start.11 = (f32[4,5376]{1,0:T(4,128)S(1)}, f32[4,5376]{1,0:T(4,128)}, u32[]{:S(2)}) copy-start(f32[4,5376]{1,0:T(4,128)} %param.20) | copy-start | bytes 258052
  7.2 8.1 %copy-start.3 = (bf16[1,256,5120]{2,1,0:T(8,128)(2,1)S(1)}, bf16[1,256,5120]{2,1,0:T(8,128)(2,1)}, u32[]{:S(2)}) copy-start(bf16[1,256,5120]{2,1,0:T(8,128)(2,1)} %param.14) | copy-start | bytes 7864324
  7.3 8.1 %copy-start.9 = (bf16[1,256,128]{2,1,0:T(8,128)(2,1)S(1)}, bf16[1,256,128]{2,1,0:T(8,128)(2,1)}, u32[]{:S(2)}) copy-start(bf16[1,256,128]{2,1,0:T(8,128)(2,1)} %param.17) | copy-start | bytes 196612
  7.3 8.1 %copy-start.10 = (bf16[1,256,128]{2,1,0:T(8,128)(2,1)S(1)}, bf16[1,256,128]{2,1,0:T(8,128)(2,1)}, u32[]{:S(2)}) copy-start(bf16[1,256,128]{2,1,0:T(8,128)(2,1)} %param.16) | copy-start | bytes 196612
  9.5 5.8 %collective-permute-start = (bf16[3,5376]{1,0:T(4,128)(2,1)S(1)}, bf16[3,5376]{1,0:T(4,128)(2,1)S(1)}, u32[]{:S(2)}, u32[]{:S(2)}) collective-permute-start(bf16[3,5376]{1,0:T(4,128)(2,1)S(1)} %slice.104), channel_id=1, source_target_pairs={{0,1},{1,2},{2,3},{3,4},{4,5},{5,6},{6,7},{7,8},{8,9},{9,10},{10,1... | collective-permute-start | bytes 96776 | tf_op jit(solution)/shard_map/ppermute | solution.py:13
  15.3 2.4 copy-start.4
  15.3 2.4 copy-start.16
  22.2 146.1 %copy-start.1 = (bf16[256,5376]{1,0:T(8,128)(2,1)}, bf16[256,5376]{1,0:T(8,128)(2,1)S(1)}, u32[]{:S(2)}) copy-start(bf16[256,5376]{1,0:T(8,128)(2,1)S(1)} %multiply_convert_fusion) | copy-start | bytes 8257540
  29.0 5.4 %copy-start.7 = (bf16[128,5120]{0,1:T(8,128)(2,1)S(1)}, bf16[128,5120]{0,1:T(8,128)(2,1)}, u32[]{:S(2)}) copy-start(bf16[128,5120]{0,1:T(8,128)(2,1)} %copy.32) | copy-start | bytes 3932164
  33.0 1.5 copy-start.5
  38.5 1.6 copy-start.18
  38.5 129.6 %copy-start.17 = (f32[80]{0:T(128)S(1)}, f32[80]{0:T(128)}, u32[]{:S(2)}) copy-start(f32[80]{0:T(128)} %param.22) | copy-start | bytes 964
  38.5 293.9 %all-gather.6.cloned.1.call-start = ((), (), s32[]{:S(2)}) async-start(), calls=%async_computation.1 | async-start | bytes 2949120 | tf_op jit(solution)/shard_map/all_gather | solution.py:130
  39.3 413.5 %all-gather.8.cloned.1.call-start = ((), (), s32[]{:S(2)}) async-start(), calls=%async_computation.2 | async-start | bytes 2105344 | tf_op jit(solution)/shard_map/all_gather | solution.py:147
  168.5 4.6 copy-start.8
  309.4 3.4 copy-start.2
  312.8 7.6 %copy-start.12 = (f32[5120]{0:T(1024)S(1)}, f32[5120]{0:T(1024)}, u32[]{:S(2)}) copy-start(f32[5120]{0:T(1024)} %param.23) | copy-start | bytes 61444
  318.1 2.3 copy-start
  334.7 127.2 %copy-start.15 = (f32[8,256]{1,0:T(8,128)}, f32[8,256]{1,0:T(8,128)S(1)}, u32[]{:S(2)}) copy-start(f32[8,256]{1,0:T(8,128)S(1)} %get-tuple-element.82) | copy-start | bytes 24580
  336.2 123.3 %all-to-all-start = ((f32[256,8,256]{2,1,0:T(8,128)}), f32[256,8,256]{2,1,0:T(8,128)S(1)}, u32[]{:S(2)}, u32[]{:S(2)}) async-start(f32[256,8,256]{2,1,0:T(8,128)} %stack.2), calls=%async_computation | async-start | bytes 4194304 | tf_op jit(solution)/shard_map/all_to_all | solution.py:136
  459.5 2.4 copy-start.6
Sparse Core Ops, SparseCore 0:
  38.6 254.3 all-gather.9
  294.8 37.4 all-gather.5
  336.1 116.6 all-gather.7
